TPU v7x, 32 devices: a whole 2x2x4 slice. The times are simulated.
32 devices in a mesh: dp: 8 (over y, x, core), tensor: 4 (over z).
Axes of the slice: x: 2, y: 2, z: 4, core: 2. Of those that a mesh axis runs over, the one named last changes fastest.
Arguments:
- teacher_master: float32 [256, 16384], P('dp', 'tensor'), as said below
- student_weight: bfloat16 [256, 16384], P('dp', 'tensor'), may hold values from -6 to 6
- teacher_feat: bfloat16 [2048, 256], P('dp'), as said below
- student_feat: bfloat16 [2048, 256], P('dp'), may hold values from -6 to 6
- center: float32 [16384], P('tensor'), may hold values from -0.3 to 0.3
Outputs:
- master_new: float32 [256, 16384], P('dp', 'tensor')
- student_grad: float32 [256, 16384], P('dp', 'tensor')
- new_center: float32 [16384], P('tensor')
Inputs may be any that keep to these rules, and one draw needn't show every extreme that they name: `teacher_feat`: rows of teacher features are real-valued and of order one. `teacher_master`: entries of the teacher master are real-valued and of order one.
All inputs are finite; a program needn't handle non-finite values.
Results may differ from a plain program's by a relative error of at most 0.014.
Values may be sent and summed in bfloat16 or wider, within the bound.
No kernel may reach another device: no remote copies, remote signals or barrier semaphores. Data moves between devices by JAX's collectives and lax.ppermute only.
A program may use at most 64 MiB of HBM per device.

v0:
```python
import jax
import jax.numpy as jnp
from jax import lax
from jax.sharding import PartitionSpec as P


def unit_rows(feat):
    wide = feat.astype(jnp.float32)
    return (wide * lax.rsqrt(jnp.sum(wide * wide, 1, keepdims=True) + 1e-06)).astype(jnp.bfloat16)


def weight_plan(teacher_master, student_weight, teacher_feat, student_feat, center):
    zt = unit_rows(teacher_feat)
    zs = unit_rows(student_feat)
    images_all = teacher_feat.shape[0] * lax.axis_size("dp")
    student_full = lax.all_gather(student_weight, "dp", axis=0, tiled=True)
    master_new = 0.996 * teacher_master + 0.004 * student_weight.astype(jnp.float32)
    weight = lax.all_gather(master_new.astype(jnp.bfloat16), "dp", axis=0, tiled=True)
    raw = jnp.dot(zt, weight, preferred_element_type=jnp.float32)
    t_norm = jnp.sqrt(jnp.sum(jnp.square(weight.astype(jnp.float32)), 0) + 1e-06)
    t_cos = raw / t_norm
    s_norm = jnp.sqrt(jnp.sum(jnp.square(student_full.astype(jnp.float32)), 0) + 1e-06)
    s_cos = jnp.dot(zs, student_full, preferred_element_type=jnp.float32) / s_norm
    t_exp = jnp.exp((t_cos - center) / 0.04)
    s_exp = jnp.exp(s_cos / 0.1)
    t_total, s_total = lax.psum(
        (jnp.sum(t_exp, 1, keepdims=True), jnp.sum(s_exp, 1, keepdims=True)), "tensor"
    )
    cos_mean = lax.psum(jnp.sum(t_cos, 0), "dp") / images_all
    new_center = 0.5 * center + 0.5 * cos_mean
    dlog = ((s_exp / s_total - t_exp / t_total) / 0.1).astype(jnp.bfloat16)
    scaled = jnp.sum(dlog.astype(jnp.float32) * s_cos, 0) / s_norm
    product = lax.dot_general(
        zs, dlog, (((0,), (0,)), ((), ())), preferred_element_type=jnp.float32
    )
    student_grad = lax.psum_scatter(
        (product - student_full.astype(jnp.float32) * scaled) / s_norm,
        "dp",
        scatter_dimension=0,
        tiled=True,
    )
    return (master_new, student_grad, new_center)


def feature_plan(teacher_master, student_weight, teacher_feat, student_feat, center):
    ndp = lax.axis_size("dp")
    bot = teacher_feat.shape[1]
    images_all = teacher_feat.shape[0] * ndp
    cols = center.shape[0] // ndp
    master_new = 0.996 * teacher_master + 0.004 * student_weight.astype(jnp.float32)
    both = jnp.stack([student_weight, master_new.astype(jnp.bfloat16)])
    both = lax.all_to_all(both, "dp", 2, 1, tiled=True)
    sw, tw = (both[0], both[1])
    feats = jnp.concatenate([unit_rows(teacher_feat), unit_rows(student_feat)], axis=1)
    feats = lax.all_gather(feats, "dp", axis=0, tiled=True)
    zt, zs = (feats[:, :bot], feats[:, bot:])
    c = lax.dynamic_slice_in_dim(center, lax.axis_index("dp") * cols, cols)
    t_norm = jnp.sqrt(jnp.sum(jnp.square(tw.astype(jnp.float32)), 0) + 1e-06)
    s_norm = jnp.sqrt(jnp.sum(jnp.square(sw.astype(jnp.float32)), 0) + 1e-06)
    t_cos = jnp.dot(zt, tw, preferred_element_type=jnp.float32) / t_norm
    s_cos = jnp.dot(zs, sw, preferred_element_type=jnp.float32) / s_norm
    t_exp = jnp.exp((t_cos - c) / 0.04)
    s_exp = jnp.exp(s_cos / 0.1)
    totals = lax.psum(jnp.stack([jnp.sum(t_exp, 1), jnp.sum(s_exp, 1)], axis=1), ("dp", "tensor"))
    t_total, s_total = (totals[:, 0:1], totals[:, 1:2])
    part_center = 0.5 * c + 0.5 * (jnp.sum(t_cos, 0) / images_all)
    new_center = lax.all_gather(part_center, "dp", axis=0, tiled=True)
    dlog = ((s_exp / s_total - t_exp / t_total) / 0.1).astype(jnp.bfloat16)
    scaled = jnp.sum(dlog.astype(jnp.float32) * s_cos, 0) / s_norm
    product = lax.dot_general(
        zs, dlog, (((0,), (0,)), ((), ())), preferred_element_type=jnp.float32
    )
    grad = (product - sw.astype(jnp.float32) * scaled) / s_norm
    student_grad = lax.all_to_all(grad, "dp", 0, 1, tiled=True)
    return (master_new, student_grad, new_center)


def solution(mesh):
    placed = (P("dp", "tensor"), P("dp", "tensor"), P("dp", None), P("dp", None), P("tensor"))
    return jax.shard_map(
        shards_for(mesh),
        mesh=mesh,
        in_specs=placed,
        out_specs=(P("dp", "tensor"), P("dp", "tensor"), P("tensor")),
        check_vma=False,
    )


def shards_for(mesh):
    ndp = mesh.shape["dp"]

    def shards(teacher_master, student_weight, teacher_feat, student_feat, center):
        images_all = teacher_feat.shape[0] * ndp
        cols = center.shape[0]
        if images_all < cols and cols % ndp == 0:
            return feature_plan(teacher_master, student_weight, teacher_feat, student_feat, center)
        return weight_plan(teacher_master, student_weight, teacher_feat, student_feat, center)

    return shards
```

profile of v0, /device:TPU:0, one launch (start us, length us, event | category | flops | bytes accessed | tf_op | source)
XLA Modules:
  0.0 120.3 jit_solution(14048190160954956227)
XLA Ops:
  7.2 0.0 all-gather.3.cloned.1.call-start
  7.2 1.0 fusion.6
  8.2 1.0 fusion.8
  9.3 1.1 fusion.7
  10.4 0.7 pad_maximum_fusion.1
  11.1 0.0 all-gather.3.cloned.1.call-update
  11.1 2.0 %convert_bitcast_fusion = (bf16[1,32,4096]{2,1,0:T(8,128)(2,1)S(1)}, f32[32,4096]{1,0:T(8,128)}) fusion(bf16[32,4096]{1,0:T(8,128)(2,1)} %param.6, f32[32,4096]{1,0:T(8,128)} %param.5), kind=kLoop, calls=%fused_computation.26 | loop fusion | flops 655360 | bytes 1572864 | tf_op jit(solution)/shard_map/stack | solution.py:51
  13.1 1.0 pad_maximum_fusion
  14.1 2.8 %copy.18 = bf16[2,32,4096]{1,0,2:T(2,128)(2,1)S(1)} copy(bf16[2,32,4096]{2,1,0:T(8,128)(2,1)S(1)} %pad_maximum_fusion) | data formatting | bytes 1048576 | tf_op jit(solution)/shard_map/stack | solution.py:51
  16.9 2.7 %reshape.42 = bf16[8,2,16384]{2,1,0:T(2,128)(2,1)} reshape(bf16[4096,2,32]{2,1,0:T(2,128)(2,1)S(1)} %bitcast.22) | data formatting | bytes 1048576
  19.6 5.2 %all-to-all-start = ((bf16[8,2,16384]{2,1,0:T(2,128)(2,1)}), bf16[8,2,16384]{2,1,0:T(2,128)(2,1)S(1)}, u32[]{:S(2)}, u32[]{:S(2)}) async-start(bf16[8,2,16384]{2,1,0:T(2,128)(2,1)} %reshape.42), calls=%async_computation | async-start | bytes 1048576 | tf_op jit(solution)/shard_map/all_to_all | solution.py:52
  24.7 0.8 dynamic_slice.3
  25.5 9.0 %all-to-all-done = bf16[8,2,16384]{2,1,0:T(2,128)(2,1)S(1)} async-done(((bf16[8,2,16384]{2,1,0:T(2,128)(2,1)}), bf16[8,2,16384]{2,1,0:T(2,128)(2,1)S(1)}, u32[]{:S(2)}, u32[]{:S(2)}) %all-to-all-start) | async-done | bytes 524320 | tf_op jit(solution)/shard_map/all_to_all | solution.py:52
  34.5 1.0 reshape.43
  35.5 1.3 %copy.19 = bf16[2,32,8,512]{3,1,2,0:T(8,128)(2,1)S(1)} copy(bf16[2,32,8,512]{1,0,3,2:T(2,128)(2,1)S(1)} %bitcast.23) | data formatting | bytes 1048576 | tf_op jit(solution)/shard_map/all_to_all | solution.py:52
  36.9 0.1 multiply_reduce_fusion.1
  37.1 4.8 %all-gather.3.cloned.1.call-done = bf16[2048,512]{1,0:T(8,128)(2,1)} async-done(((bf16[256,512]{1,0:T(8,128)(2,1)}), bf16[2048,512]{1,0:T(8,128)(2,1)}) %all-gather.3.cloned.1.call-update) | async-done | bytes 2097168 | tf_op jit(solution)/shard_map/all_gather | solution.py:55
  41.9 0.0 copy-start
  41.9 4.1 %fusion = (f32[2048]{0:T(1024)S(1)}, f32[2048,512]{1,0:T(8,128)}) fusion(f32[512]{0:T(512)S(1)} %get-tuple-element.22, bf16[256,512]{1,0:T(8,128)(2,1)S(1)} %bitcast.29, bf16[2048,512]{1,0:T(8,128)(2,1)} %all-gather.3.cloned.1.call-done), kind=kOutput, calls=%fused_computation.4 | convolution fusion | flops 540014592 | bytes 5515264 | tf_op jit(solution)/shard_map/dot_general | solution.py:61
  46.0 0.0 copy-done
  46.0 3.1 %fusion.10 = (f32[512]{0:T(512)S(1)}, f32[2048]{0:T(1024)S(1)}, f32[2048,512]{1,0:T(8,128)}) fusion(f32[512]{0:T(512)S(1)} %dynamic_slice.3, f32[512]{0:T(512)S(1)} %get-tuple-element.21, bf16[256,512]{1,0:T(8,128)(2,1)S(1)} %bitcast.31, bf16[2048,512]{1,0:T(8,128)(2,1)S(1)} %copy-done), kind=kOutput, calls=%fused_computation.34 | convolution fusion | flops 542111232 | bytes 5519360 | tf_op jit(solution)/shard_map/dot_general | solution.py:60
  49.2 39.5 %psum.7 = f32[2048,2]{0,1:T(2,128)S(1)} all-reduce(f32[2048,2]{0,1:T(2,128)S(1)} %pad_maximum_fusion.2), channel_id=1, replica_groups=mesh['dp'=8,'tensor'=4] {'dp','tensor'}, use_global_device_ids=true, to_apply=%region_6.0 | all-reduce | flops 4096 | bytes 32768 | tf_op jit(solution)/shard_map/psum | solution.py:64
  88.7 4.5 %multiply_reduce_fusion = (f32[512]{0:T(512)S(1)}, bf16[2048,512]{1,0:T(8,128)(2,1)S(1)}) fusion(f32[2048,512]{1,0:T(8,128)} %get-tuple-element.19, f32[2048]{0:T(1024)S(1)} %bitcast.34, f32[2048,512]{1,0:T(8,128)} %get-tuple-element.20, f32[512]{0:T(512)S(1)} %dynamic_slice.3, f32[2048]{0:T(1024)S(1)} %bitcast.33), kind=kLoop, calls=%fused_computation | loop fusion | flops 11533824 | bytes 10506240 | tf_op jit(solution)/shard_map/reduce_sum | solution.py:69
  93.2 1.5 %fusion.2 = f32[256,512]{1,0:T(8,128)} fusion(bf16[2048,512]{1,0:T(8,128)(2,1)S(1)} %get-tuple-element.11, bf16[2048,512]{1,0:T(8,128)(2,1)S(1)} %copy-done, bf16[256,512]{1,0:T(8,128)(2,1)S(1)} %bitcast.30, f32[512]{0:T(512)S(1)} %get-tuple-element.22, f32[512]{0:T(512)S(1)} %rsqrt_multiply_fusion), kind=kOutput, calls=%fused_computation.9 | convolution fusion | flops 537395200 | bytes 3936256 | tf_op jit(solution)/shard_map/dot_general | solution.py:70
  94.8 4.4 %all-to-all-start.1 = ((f32[8,32,512]{2,1,0:T(8,128)}), f32[8,32,512]{2,1,0:T(8,128)S(1)}, u32[]{:S(2)}, u32[]{:S(2)}) async-start(f32[8,32,512]{2,1,0:T(8,128)} %bitcast.10), calls=%async_computation.1 | async-start | bytes 1048576 | tf_op jit(solution)/shard_map/all_to_all | solution.py:74
  99.2 0.8 multiply_add_fusion.1
  99.9 12.1 %all-gather = f32[8,1,512]{2,1,0:T(1,128)S(1)} all-gather(f32[1,1,512]{2,1,0:T(1,128)S(1)} %bitcast.35), channel_id=1, replica_groups=mesh['dp'=8,'tensor'=4] {'dp'}, dimensions={0}, use_global_device_ids=true | all-gather | bytes 18432 | tf_op jit(solution)/shard_map/all_gather | solution.py:67
  112.0 0.0 all-to-all-done.1
  112.0 0.8 copy.21
  112.8 0.6 copy.23
  (7 shorter events, 0.1 us)
Async XLA Ops:
  7.2 34.7 %all-gather.3.cloned.1.call-start = ((), (), s32[]{:S(2)}) async-start(), calls=%async_computation.2 | async-start | bytes 2359296 | tf_op jit(solution)/shard_map/all_gather | solution.py:55
  19.6 14.9 %all-to-all-start = ((bf16[8,2,16384]{2,1,0:T(2,128)(2,1)}), bf16[8,2,16384]{2,1,0:T(2,128)(2,1)S(1)}, u32[]{:S(2)}, u32[]{:S(2)}) async-start(bf16[8,2,16384]{2,1,0:T(2,128)(2,1)} %reshape.42), calls=%async_computation | async-start | bytes 1048576 | tf_op jit(solution)/shard_map/all_to_all | solution.py:52
  41.9 4.1 %copy-start = (bf16[2048,512]{1,0:T(8,128)(2,1)S(1)}, bf16[2048,512]{1,0:T(8,128)(2,1)}, u32[]{:S(2)}) copy-start(bf16[2048,512]{1,0:T(8,128)(2,1)} %all-gather.3.cloned.1.call-done) | copy-start | bytes 6291460
  94.8 17.2 %all-to-all-start.1 = ((f32[8,32,512]{2,1,0:T(8,128)}), f32[8,32,512]{2,1,0:T(8,128)S(1)}, u32[]{:S(2)}, u32[]{:S(2)}) async-start(f32[8,32,512]{2,1,0:T(8,128)} %bitcast.10), calls=%async_computation.1 | async-start | bytes 1048576 | tf_op jit(solution)/shard_map/all_to_all | solution.py:74
Sparse Core Ops, SparseCore 0:
  11.2 30.5 all-gather.2
where the time goes:
time: 121 us; the launch traced here: 120 us
  blocking collectives  51.6 us (43%)
  between operations  14.1 us (12%)
  waiting for transfers between devices  13.8 us (11%)
  other arithmetic  12.3 us (10%)
  local copies, waits for them, and re-layouts  10.1 us (8%)
  starting transfers between devices  9.6 us (8%)
  matrix products  8.79 us (7%)
    psum x1, blocking collectives, feature_plan(): lax.psum(jnp.stack([jnp.sum(t_exp, 1), jnp.sum(s_exp, 1)], axis=1), ('dp'...  39.5 us
    all_gather x1, blocking collectives, feature_plan(): new_center = lax.all_gather(part_center, 'dp', axis=0, tiled=True)  12.1 us
    all_to_all x1, waiting for transfers between devices, feature_plan(): both = lax.all_to_all(both, 'dp', 2, 1, tiled=True)  8.99 us
    all_to_all x1, starting transfers between devices, feature_plan(): both = lax.all_to_all(both, 'dp', 2, 1, tiled=True)  5.17 us
    all_gather x1, waiting for transfers between devices, feature_plan(): feats = lax.all_gather(feats, 'dp', axis=0, tiled=True)  4.81 us
    reduce_sum x1, other arithmetic, feature_plan(): scaled = jnp.sum(dlog.astype(jnp.float32) * s_cos, 0) / s_norm  4.52 us
    all_to_all x1, starting transfers between devices, feature_plan(): student_grad = lax.all_to_all(grad, 'dp', 0, 1, tiled=True)  4.39 us
    unnamed x5, local copies, waits for them, and re-layouts  4.31 us
  transfers between devices with their start and end apart: 3, of which 2 were waited for; matrix products, arithmetic and copies ran while one was open for 10% of the time, Pallas kernels for 0%

commit v1 on v0

--- a/solution.py
+++ b/solution.py
@@ -52,7 +52,12 @@
     both = lax.all_to_all(both, "dp", 2, 1, tiled=True)
     sw, tw = (both[0], both[1])
     feats = jnp.concatenate([unit_rows(teacher_feat), unit_rows(student_feat)], axis=1)
-    feats = lax.all_gather(feats, "dp", axis=0, tiled=True)
+    ring = [feats]
+    for hop in range(7):
+        ring.append(lax.ppermute(ring[-1], "dp", [(dev, (dev + 1) % 8) for dev in range(8)]))
+    feats = jnp.roll(
+        jnp.concatenate(ring[::-1], axis=0), (lax.axis_index("dp") + 1) * ring[0].shape[0], axis=0
+    )
     zt, zs = (feats[:, :bot], feats[:, bot:])
     c = lax.dynamic_slice_in_dim(center, lax.axis_index("dp") * cols, cols)
     t_norm = jnp.sqrt(jnp.sum(jnp.square(tw.astype(jnp.float32)), 0) + 1e-06)

time: 121 us -> 143 us (1.18)
  waiting for transfers between devices: 13.8 us -> 41.2 us
  between operations: 14.1 us -> 0.84 us
  local copies, waits for them, and re-layouts: 10.1 us -> 17.9 us
    ppermute x0 -> x7, waiting for transfers between devices: none -> 41.2 us  [feature_plan(): lax.ppermute(ring[-1], 'dp', [(dev, (dev + 1) % 8) for dev in range(8)])]
    all_to_all x1, waiting for transfers between devices: 8.99 us -> 0.01 us  [feature_plan(): both = lax.all_to_all(both, 'dp', 2, 1, tiled=True)]
    unnamed x5 -> x19, local copies, waits for them, and re-layouts: 4.31 us -> 12.2 us
    all_gather x1 -> x0, waiting for transfers between devices: 4.81 us -> none  [feature_plan(): feats = lax.all_gather(feats, 'dp', axis=0, tiled=True)]
  transfers between devices with their start and end apart: 3 -> 9, of which waited for: 2 -> 6; matrix products, arithmetic and copies ran while one was open for 10% -> 9% of each run, Pallas kernels for 0% -> 0%
where the time goes in v1:
time: 143 us; the launch traced here: 142 us
  blocking collectives  51.7 us (36%)
  waiting for transfers between devices  41.2 us (29%)
  local copies, waits for them, and re-layouts  17.9 us (13%)
  other arithmetic  11.6 us (8%)
  starting transfers between devices  9.69 us (7%)
  matrix products  9.08 us (6%)
    ppermute x7, waiting for transfers between devices, feature_plan(): lax.ppermute(ring[-1], 'dp', [(dev, (dev + 1) % 8) for dev in range(8)])  41.2 us
    psum x1, blocking collectives, feature_plan(): lax.psum(jnp.stack([jnp.sum(t_exp, 1), jnp.sum(s_exp, 1)], axis=1), ('dp'...  39.7 us
    unnamed x19, local copies, waits for them, and re-layouts  12.2 us
    all_gather x1, blocking collectives, feature_plan(): new_center = lax.all_gather(part_center, 'dp', axis=0, tiled=True)  12.1 us
    all_to_all x1, starting transfers between devices, feature_plan(): both = lax.all_to_all(both, 'dp', 2, 1, tiled=True)  4.73 us
    reduce_sum x1, other arithmetic, feature_plan(): scaled = jnp.sum(dlog.astype(jnp.float32) * s_cos, 0) / s_norm  4.52 us
    all_to_all x1, starting transfers between devices, feature_plan(): student_grad = lax.all_to_all(grad, 'dp', 0, 1, tiled=True)  3.94 us
    dot_general x1, matrix products, feature_plan(): s_cos = jnp.dot(zs, sw, preferred_element_type=jnp.float32) / s_norm  3.21 us
  transfers between devices with their start and end apart: 9, of which 6 were waited for; matrix products, arithmetic and copies ran while one was open for 9% of the time, Pallas kernels for 0%

profile of v1, /device:TPU:0, one launch (start us, length us, event | category | flops | bytes accessed | tf_op | source)
XLA Modules:
  0.0 142.1 jit_solution(14228443467287470027)
XLA Ops:
  0.6 1.0 fusion.6
  1.7 1.0 fusion.8
  2.7 1.1 fusion.7
  3.8 0.5 collective-permute-start
  4.3 6.9 %collective-permute-done = bf16[256,512]{1,0:T(8,128)(2,1)S(1)} collective-permute-done((bf16[256,512]{1,0:T(8,128)(2,1)S(1)}, bf16[256,512]{1,0:T(8,128)(2,1)S(1)}, u32[]{:S(2)}, u32[]{:S(2)}) %collective-permute-start) | collective-permute-done | bytes 262176 | tf_op jit(solution)/shard_map/ppermute | solution.py:57
  11.3 0.0 collective-permute-start.1
  11.3 6.7 %collective-permute-done.1 = bf16[256,512]{1,0:T(8,128)(2,1)S(1)} collective-permute-done((bf16[256,512]{1,0:T(8,128)(2,1)S(1)}, bf16[256,512]{1,0:T(8,128)(2,1)S(1)}, u32[]{:S(2)}, u32[]{:S(2)}) %collective-permute-start.1) | collective-permute-done | bytes 262176 | tf_op jit(solution)/shard_map/ppermute | solution.py:57
  18.0 0.0 collective-permute-start.2
  18.0 2.0 %convert_bitcast_fusion = (bf16[1,32,4096]{2,1,0:T(8,128)(2,1)S(1)}, f32[32,4096]{1,0:T(8,128)}) fusion(bf16[32,4096]{1,0:T(8,128)(2,1)} %param.6, f32[32,4096]{1,0:T(8,128)} %param.5), kind=kLoop, calls=%fused_computation.26 | loop fusion | flops 655360 | bytes 1572864 | tf_op jit(solution)/shard_map/stack | solution.py:51
  20.0 4.8 %collective-permute-done.2 = bf16[256,512]{1,0:T(8,128)(2,1)} collective-permute-done((bf16[256,512]{1,0:T(8,128)(2,1)S(1)}, bf16[256,512]{1,0:T(8,128)(2,1)}, u32[]{:S(2)}, u32[]{:S(2)}) %collective-permute-start.2) | collective-permute-done | bytes 262176 | tf_op jit(solution)/shard_map/ppermute | solution.py:57
  24.8 0.0 collective-permute-start.3
  24.8 1.0 pad_maximum_fusion
  25.8 2.8 %copy.18 = bf16[2,32,4096]{1,0,2:T(2,128)(2,1)S(1)} copy(bf16[2,32,4096]{2,1,0:T(8,128)(2,1)S(1)} %pad_maximum_fusion) | data formatting | bytes 1048576 | tf_op jit(solution)/shard_map/stack | solution.py:51
  28.6 2.7 %reshape.42 = bf16[8,2,16384]{2,1,0:T(2,128)(2,1)} reshape(bf16[4096,2,32]{2,1,0:T(2,128)(2,1)S(1)} %bitcast.22) | data formatting | bytes 1048576
  31.2 4.7 %all-to-all-start = ((bf16[8,2,16384]{2,1,0:T(2,128)(2,1)}), bf16[8,2,16384]{2,1,0:T(2,128)(2,1)S(1)}, u32[]{:S(2)}, u32[]{:S(2)}) async-start(bf16[8,2,16384]{2,1,0:T(2,128)(2,1)} %reshape.42), calls=%async_computation | async-start | bytes 1048576 | tf_op jit(solution)/shard_map/all_to_all | solution.py:52
  36.0 0.0 collective-permute-done.3
  36.0 0.5 collective-permute-start.4
  36.5 12.1 %collective-permute-done.4 = bf16[256,512]{1,0:T(8,128)(2,1)} collective-permute-done((bf16[256,512]{1,0:T(8,128)(2,1)}, bf16[256,512]{1,0:T(8,128)(2,1)}, u32[]{:S(2)}, u32[]{:S(2)}) %collective-permute-start.4) | collective-permute-done | bytes 262176 | tf_op jit(solution)/shard_map/ppermute | solution.py:57
  48.6 0.0 collective-permute-start.5
  48.6 0.8 dynamic_slice.8
  49.4 0.0 all-to-all-done
  49.4 1.0 reshape.43
  50.4 1.3 copy.19
  51.7 0.1 multiply_reduce_fusion.1
  51.9 3.8 %collective-permute-done.5 = bf16[256,512]{1,0:T(8,128)(2,1)} collective-permute-done((bf16[256,512]{1,0:T(8,128)(2,1)}, bf16[256,512]{1,0:T(8,128)(2,1)}, u32[]{:S(2)}, u32[]{:S(2)}) %collective-permute-start.5) | collective-permute-done | bytes 262176 | tf_op jit(solution)/shard_map/ppermute | solution.py:57
  55.6 0.0 collective-permute-start.6
  55.7 6.8 %collective-permute-done.6 = bf16[256,512]{1,0:T(8,128)(2,1)S(1)} collective-permute-done((bf16[256,512]{1,0:T(8,128)(2,1)}, bf16[256,512]{1,0:T(8,128)(2,1)S(1)}, u32[]{:S(2)}, u32[]{:S(2)}) %collective-permute-start.6) | collective-permute-done | bytes 262176 | tf_op jit(solution)/shard_map/ppermute | solution.py:57
  62.6 1.0 constant_dynamic-update-slice_fusion.14
  63.5 1.0 constant_dynamic-update-slice_fusion.13
  64.5 1.0 constant_dynamic-update-slice_fusion.12
  65.5 1.0 constant_dynamic-update-slice_fusion.11
  66.6 1.0 constant_dynamic-update-slice_fusion.6
  67.5 1.0 constant_dynamic-update-slice_fusion.5
  68.5 1.0 constant_dynamic-update-slice_fusion.4
  69.5 1.0 constant_dynamic-update-slice_fusion.3
  70.5 0.0 copy-start
  70.5 3.2 %fusion = (f32[2048]{0:T(1024)S(1)}, f32[2048,512]{1,0:T(8,128)}) fusion(f32[512]{0:T(512)S(1)} %get-tuple-element.22, bf16[256,512]{1,0:T(8,128)(2,1)S(1)} %bitcast.29, bf16[4096,512]{1,0:T(8,128)(2,1)S(1)} %constant_dynamic-update-slice_fusion, s32[]{:T(128)S(6)} %select_n.17, s32[]{:T(128)S(6)} %add.67), kind=kOutput, calls=%fused_computation.4 | convolution fusion | flops 540014592 | bytes 5515272 | tf_op jit(solution)/shard_map/dot_general | solution.py:66
  73.8 0.0 copy-done
  73.8 3.1 %fusion.11 = (f32[512]{0:T(512)S(1)}, f32[2048]{0:T(1024)S(1)}, f32[2048,512]{1,0:T(8,128)}) fusion(f32[512]{0:T(512)S(1)} %dynamic_slice.8, f32[512]{0:T(512)S(1)} %get-tuple-element.21, bf16[256,512]{1,0:T(8,128)(2,1)S(1)} %bitcast.31, bf16[4096,512]{1,0:T(8,128)(2,1)S(1)} %constant_dynamic-update-slice_fusion, s32[]{:T(128)S(6)} %select_n.17), kind=kOutput, calls=%fused_computation.51 | convolution fusion | flops 542111232 | bytes 5519364 | tf_op jit(solution)/shard_map/dot_general | solution.py:65
  76.9 39.7 %psum.7 = f32[2048,2]{0,1:T(2,128)S(1)} all-reduce(f32[2048,2]{0,1:T(2,128)S(1)} %pad_maximum_fusion.2), channel_id=1, replica_groups=mesh['dp'=8,'tensor'=4] {'dp','tensor'}, use_global_device_ids=true, to_apply=%region_6.7 | all-reduce | flops 4096 | bytes 32768 | tf_op jit(solution)/shard_map/psum | solution.py:69
  116.6 4.5 %multiply_reduce_fusion = (f32[512]{0:T(512)S(1)}, bf16[2048,512]{1,0:T(8,128)(2,1)S(1)}) fusion(f32[2048,512]{1,0:T(8,128)} %get-tuple-element.19, f32[2048]{0:T(1024)S(1)} %bitcast.34, f32[2048,512]{1,0:T(8,128)} %get-tuple-element.20, f32[512]{0:T(512)S(1)} %dynamic_slice.8, f32[2048]{0:T(1024)S(1)} %bitcast.33), kind=kLoop, calls=%fused_computation | loop fusion | flops 11533824 | bytes 10506240 | tf_op jit(solution)/shard_map/reduce_sum | solution.py:74
  121.1 2.8 %fusion.2 = f32[256,512]{1,0:T(8,128)} fusion(bf16[2048,512]{1,0:T(8,128)(2,1)S(1)} %get-tuple-element.11, bf16[4096,512]{1,0:T(8,128)(2,1)} %copy-done, s32[]{:T(128)S(6)} %select_n.17, s32[]{:T(128)S(6)} %add.67, bf16[256,512]{1,0:T(8,128)(2,1)S(1)} %bitcast.30, f32[512]{0:T(512)S(1)} %get-tuple-element.22, f32[512]{0:T(512)S(1)} %rsqrt_multiply_fusion), kind=kOutput, calls=%fused_computation.9 | convolution fusion | flops 537395200 | bytes 3936264 | tf_op jit(solution)/shard_map/dot_general | solution.py:75
  123.9 3.9 %all-to-all-start.1 = ((f32[8,32,512]{2,1,0:T(8,128)}), f32[8,32,512]{2,1,0:T(8,128)S(1)}, u32[]{:S(2)}, u32[]{:S(2)}) async-start(f32[8,32,512]{2,1,0:T(8,128)} %bitcast.10), calls=%async_computation.1 | async-start | bytes 1048576 | tf_op jit(solution)/shard_map/all_to_all | solution.py:79
  127.8 0.8 multiply_add_fusion.1
  128.6 12.1 %all-gather = f32[8,1,512]{2,1,0:T(1,128)S(1)} all-gather(f32[1,1,512]{2,1,0:T(1,128)S(1)} %bitcast.35), channel_id=1, replica_groups=mesh['dp'=8,'tensor'=4] {'dp'}, dimensions={0}, use_global_device_ids=true | all-gather | bytes 18432 | tf_op jit(solution)/shard_map/all_gather | solution.py:72
  140.6 0.0 all-to-all-done.1
  140.6 0.8 copy.21
  141.5 0.6 copy.38
  (16 shorter events, 0.3 us)
Async XLA Ops:
  3.8 7.4 %collective-permute-start = (bf16[256,512]{1,0:T(8,128)(2,1)S(1)}, bf16[256,512]{1,0:T(8,128)(2,1)S(1)}, u32[]{:S(2)}, u32[]{:S(2)}) collective-permute-start(bf16[256,512]{1,0:T(8,128)(2,1)S(1)} %pad_maximum_fusion.1), channel_id=1, source_target_pairs={{0,4},{4,8},{8,12},{12,16},{16,20},{20,24},{24,28},{28,0},{1,5},{5... | collective-permute-start | bytes 786440 | tf_op jit(solution)/shard_map/ppermute | solution.py:57
  11.3 6.7 %collective-permute-start.1 = (bf16[256,512]{1,0:T(8,128)(2,1)S(1)}, bf16[256,512]{1,0:T(8,128)(2,1)S(1)}, u32[]{:S(2)}, u32[]{:S(2)}) collective-permute-start(bf16[256,512]{1,0:T(8,128)(2,1)S(1)} %collective-permute-done), channel_id=1, source_target_pairs={{0,4},{4,8},{8,12},{12,16},{16,20},{20,24},{24,28},{28,0},{1,5},{5... | collective-permute-start | bytes 786440 | tf_op jit(solution)/shard_map/ppermute | solution.py:57
  18.0 6.8 %collective-permute-start.2 = (bf16[256,512]{1,0:T(8,128)(2,1)S(1)}, bf16[256,512]{1,0:T(8,128)(2,1)}, u32[]{:S(2)}, u32[]{:S(2)}) collective-permute-start(bf16[256,512]{1,0:T(8,128)(2,1)S(1)} %collective-permute-done.1), channel_id=1, source_target_pairs={{0,4},{4,8},{8,12},{12,16},{16,20},{20,24},{24,28},{28,0},{1,5},{5... | collective-permute-start | bytes 786440 | tf_op jit(solution)/shard_map/ppermute | solution.py:57
  24.8 11.2 %collective-permute-start.3 = (bf16[256,512]{1,0:T(8,128)(2,1)}, bf16[256,512]{1,0:T(8,128)(2,1)}, u32[]{:S(2)}, u32[]{:S(2)}) collective-permute-start(bf16[256,512]{1,0:T(8,128)(2,1)} %collective-permute-done.2), channel_id=1, source_target_pairs={{0,4},{4,8},{8,12},{12,16},{16,20},{20,24},{24,28},{28,0},{1,5},{5... | collective-permute-start | bytes 786440 | tf_op jit(solution)/shard_map/ppermute | solution.py:57
  31.2 18.2 %all-to-all-start = ((bf16[8,2,16384]{2,1,0:T(2,128)(2,1)}), bf16[8,2,16384]{2,1,0:T(2,128)(2,1)S(1)}, u32[]{:S(2)}, u32[]{:S(2)}) async-start(bf16[8,2,16384]{2,1,0:T(2,128)(2,1)} %reshape.42), calls=%async_computation | async-start | bytes 1048576 | tf_op jit(solution)/shard_map/all_to_all | solution.py:52
  36.0 12.7 %collective-permute-start.4 = (bf16[256,512]{1,0:T(8,128)(2,1)}, bf16[256,512]{1,0:T(8,128)(2,1)}, u32[]{:S(2)}, u32[]{:S(2)}) collective-permute-start(bf16[256,512]{1,0:T(8,128)(2,1)} %collective-permute-done.3), channel_id=1, source_target_pairs={{0,4},{4,8},{8,12},{12,16},{16,20},{20,24},{24,28},{28,0},{1,5},{5... | collective-permute-start | bytes 786440 | tf_op jit(solution)/shard_map/ppermute | solution.py:57
  48.6 7.0 %collective-permute-start.5 = (bf16[256,512]{1,0:T(8,128)(2,1)}, bf16[256,512]{1,0:T(8,128)(2,1)}, u32[]{:S(2)}, u32[]{:S(2)}) collective-permute-start(bf16[256,512]{1,0:T(8,128)(2,1)} %collective-permute-done.4), channel_id=1, source_target_pairs={{0,4},{4,8},{8,12},{12,16},{16,20},{20,24},{24,28},{28,0},{1,5},{5... | collective-permute-start | bytes 786440 | tf_op jit(solution)/shard_map/ppermute | solution.py:57
  55.6 6.9 %collective-permute-start.6 = (bf16[256,512]{1,0:T(8,128)(2,1)}, bf16[256,512]{1,0:T(8,128)(2,1)S(1)}, u32[]{:S(2)}, u32[]{:S(2)}) collective-permute-start(bf16[256,512]{1,0:T(8,128)(2,1)} %collective-permute-done.5), channel_id=1, source_target_pairs={{0,4},{4,8},{8,12},{12,16},{16,20},{20,24},{24,28},{28,0},{1,5},{5... | collective-permute-start | bytes 786440 | tf_op jit(solution)/shard_map/ppermute | solution.py:57
  70.5 3.2 %copy-start = (bf16[4096,512]{1,0:T(8,128)(2,1)}, bf16[4096,512]{1,0:T(8,128)(2,1)S(1)}, u32[]{:S(2)}) copy-start(bf16[4096,512]{1,0:T(8,128)(2,1)S(1)} %constant_dynamic-update-slice_fusion) | copy-start | bytes 12582916
  123.9 16.8 %all-to-all-start.1 = ((f32[8,32,512]{2,1,0:T(8,128)}), f32[8,32,512]{2,1,0:T(8,128)S(1)}, u32[]{:S(2)}, u32[]{:S(2)}) async-start(f32[8,32,512]{2,1,0:T(8,128)} %bitcast.10), calls=%async_computation.1 | async-start | bytes 1048576 | tf_op jit(solution)/shard_map/all_to_all | solution.py:79
